TPU v7x, 32 devices: a whole 2x2x4 slice. The times are simulated.
32 devices in a mesh: grp: 2 (over y), cell: 8 (over z, x), gene: 2 (over core).
Axes of the slice: x: 2, y: 2, z: 4, core: 2. Of those that a mesh axis runs over, the one named last changes fastest.
Arguments:
- expression: bfloat16 [2048, 16384], P(('grp', 'cell'), 'gene'), parts along dimension 0, may hold values from -6 to 6
- design: bfloat16 [2048, 128], P(('grp', 'cell')), parts along dimension 0, may hold values from -24 to 24
- quantile_level: float32 [16384], P('gene'), may hold values from 0.1 to 0.9
Outputs:
- quantile_slack: bfloat16 [2048, 16384], P(('grp', 'cell'), 'gene'), parts along dimension 0
- low_rank_coef: float32 [32768, 128], P(('grp', 'gene', 'cell')), parts along dimension 0
There are 2 independent parts, one for each index of `grp`. A program takes and returns all parts, laid end to end along the dimension named above; an argument that names none is the same for every part. Nothing has to cross between parts.
All inputs are finite; a program needn't handle non-finite values.
Results may differ from a plain program's by a relative error of at most 0.0025.
The roundings to bfloat16 on the way count: a program that leaves them out, or rounds other values in their place, can miss the bound.
Values may be sent and summed in bfloat16 or wider, within the bound.
No kernel may reach another device: no remote copies, remote signals or barrier semaphores. Data moves between devices by JAX's collectives and lax.ppermute only.
A program may use at most 64 MiB of HBM per device.

v0:
```python
import math
import jax
import jax.numpy as jnp
from jax import lax
from jax.sharding import PartitionSpec as P

NS_STEPS = 8
shrink_rate = 0.25


def matmul(left, right):
    return jnp.dot(left, right, precision=lax.Precision.HIGHEST)


def invert(matrix):
    identity = jnp.eye(matrix.shape[0], dtype=jnp.float32)
    factor = jnp.linalg.cholesky(matrix)
    lower_inv = lax.linalg.triangular_solve(factor, identity, left_side=True, lower=True)
    return matmul(lower_inv.T, lower_inv)


def newton(moment):
    identity = jnp.eye(moment.shape[0], dtype=jnp.float32)
    current = moment / jnp.trace(moment)
    root_inv = identity
    for sweep in range(NS_STEPS):
        middle = 1.5 * identity - 0.5 * matmul(root_inv, current)
        current = matmul(current, middle)
        root_inv = matmul(middle, root_inv)
    return root_inv


def per_device(expression, design, quantile_level):
    width = design.shape[1]
    identity = jnp.eye(width, dtype=jnp.float32)
    local_gram = lax.dot_general(
        design, design, (((0,), (0,)), ((), ())), preferred_element_type=jnp.float32
    )
    crossed = lax.psum_scatter(
        lax.dot_general(
            expression, design, (((0,), (0,)), ((), ())), preferred_element_type=jnp.float32
        ),
        "cell",
        scatter_dimension=0,
        tiled=True,
    )
    gram_total = lax.psum(local_gram, "cell")
    inverse = invert(gram_total + identity)
    coef = matmul(crossed, inverse)
    local_moment = lax.dot_general(
        coef, coef, (((0,), (0,)), ((), ())), precision=lax.Precision.HIGHEST
    )
    moment = lax.psum(local_moment, ("cell", "gene"))
    root_inv = newton(moment)
    low_rank_coef = coef - shrink_rate / math.sqrt(width) * matmul(coef, root_inv)
    coef_low = coef.astype(jnp.bfloat16)
    fitted = lax.dot_general(
        design,
        lax.all_gather(coef_low, "cell", axis=0, tiled=True),
        (((1,), (1,)), ((), ())),
        preferred_element_type=jnp.float32,
    )
    slack = expression.astype(jnp.float32) - fitted
    level = quantile_level[None, :]
    quantile_slack = (slack - jnp.clip(slack, level - 1.0, level)).astype(jnp.bfloat16)
    return (quantile_slack, low_rank_coef)


def solution(mesh):
    placed = (P(("grp", "cell"), "gene"), P(("grp", "cell"), None), P("gene"))
    return jax.shard_map(
        per_device,
        mesh=mesh,
        in_specs=placed,
        out_specs=(P(("grp", "cell"), "gene"), P(("grp", "gene", "cell"), None)),
        check_vma=False,
    )
```

profile of v0, /device:TPU:0, one launch (start us, length us, event | category | flops | bytes accessed | tf_op | source)
XLA Modules:
  0.0 335.5 jit_solution(2231902465308282045)
XLA Ops:
  7.2 0.7 copy-done
  7.9 0.8 fusion.18
  8.8 4.3 %fusion.17 = f32[8192,128]{1,0:T(8,128)} fusion(bf16[128,8192]{1,0:T(8,128)(2,1)} %param.3, bf16[128,128]{1,0:T(8,128)(2,1)S(1)} %copy-done), kind=kOutput, calls=%fused_computation.38 | convolution fusion | flops 268435456 | bytes 6324224 | tf_op jit(solution)/shard_map/dot_general | solution.py:40
  13.2 0.0 all-reduce.5.cloned.1.call-start
  13.2 0.1 copy.7
  13.4 70.6 %all-reduce.3.cloned.1.call-done = f32[128,128]{0,1:T(8,128)} async-done(((f32[128,128]{0,1:T(8,128)}), f32[128,128]{0,1:T(8,128)}) %all-reduce.3.cloned.1.call-update) | async-done | bytes 65552 | tf_op jit(solution)/shard_map/psum | solution.py:47
  84.0 0.8 convert_add_fusion
  84.8 0.1 copy.8
  84.9 11.7 %cholesky.29 = f32[128,128]{1,0:T(8,128)S(1)} custom-call(f32[128,128]{1,0:T(8,128)S(1)} %fusion.13), custom_call_target="Cholesky" | custom-call | tf_op jit(solution)/shard_map/jit(cholesky)/cholesky | solution.py:17
  96.7 0.6 compare_reduce_fusion
  97.3 0.7 fusion.10
  98.0 9.8 %custom-call.6 = f32[1,128,128]{1,2,0:T(8,128)S(1)} custom-call(f32[1,128,128]{2,1,0:T(8,128)S(1)} %fusion.10), custom_call_target="InvertDiagBlocksLowerTriangular" | custom-call | tf_op jit(solution)/shard_map/triangular_solve | solution.py:18
  107.8 0.2 fusion.11
  108.0 0.3 fusion.19
  108.3 67.6 %reduce-scatter.2.cloned.1.call-done = f32[1024,128]{1,0:T(8,128)} async-done(((f32[8192,128]{1,0:T(8,128)}), f32[1024,128]{1,0:T(8,128)}) %reduce-scatter.2.cloned.1.call-update) | async-done | bytes 524304 | tf_op jit(solution)/shard_map/reduce_scatter | solution.py:39
  176.0 2.3 fusion.16
  178.3 1.6 fusion.20
  180.0 0.2 all-gather.2.cloned.1.call-start
  180.2 2.4 copy.5
  182.7 83.3 %all-reduce.5.cloned.1.call-done = f32[128,128]{1,0:T(8,128)} async-done(((f32[128,128]{1,0:T(8,128)}), f32[128,128]{1,0:T(8,128)}) %all-reduce.5.cloned.1.call-update) | async-done | bytes 65552 | tf_op jit(solution)/shard_map/psum | solution.py:53
  266.0 1.5 select_reduce_fusion
  267.5 1.7 fusion.9
  269.1 0.2 fusion.14
  269.3 1.7 fusion.15
  271.0 0.2 fusion.8
  271.2 0.2 fusion.21
  271.5 0.2 fusion.22
  271.7 0.2 fusion.7
  271.9 0.2 fusion.23
  272.1 0.2 fusion.24
  272.3 0.2 fusion.6
  272.5 0.2 fusion.25
  272.7 0.2 fusion.26
  273.0 0.2 fusion.5
  273.2 0.2 fusion.27
  273.4 0.2 fusion.28
  273.6 0.2 fusion.4
  273.8 0.2 fusion.29
  274.0 0.2 fusion.30
  274.2 0.2 fusion.3
  274.4 0.2 fusion.31
  274.6 0.2 fusion.32
  274.9 0.2 fusion.2
  275.1 0.2 fusion.33
  275.3 1.4 fusion.1
  276.6 42.0 %all-gather.2.cloned.1.call-done = bf16[8192,128]{1,0:T(8,128)(2,1)} async-done(((bf16[1024,128]{1,0:T(8,128)(2,1)}), bf16[8192,128]{1,0:T(8,128)(2,1)}) %all-gather.2.cloned.1.call-update) | async-done | bytes 2097168 | tf_op jit(solution)/shard_map/all_gather | solution.py:59
  318.7 6.2 %subtract_convert_fusion = bf16[128,8192]{0,1:T(8,128)(2,1)} fusion(bf16[8192,128]{1,0:T(8,128)(2,1)} %all-gather.2.cloned.1.call-done, bf16[128,128]{1,0:T(8,128)(2,1)S(1)} %copy-done, bf16[128,8192]{0,1:T(8,128)(2,1)S(1)} %copy-done.2, f32[8192]{0:T(1024)S(1)} %broadcast_add_fusion, f32[8192]{0:T(1024)S(1)} %copy-done.3), kind=kOutput, calls=%fused_computation.2 | convolution fusion | flops 274726912 | bytes 6389760 | tf_op jit(solution)/shard_map/dot_general | solution.py:57
  324.9 4.1 %copy.9 = bf16[128,8192]{1,0:T(8,128)(2,1)} copy(bf16[128,8192]{0,1:T(8,128)(2,1)} %subtract_convert_fusion) | data formatting | bytes 4194304
  (17 shorter events, 0.2 us)
Async XLA Ops:
  7.2 0.8 copy-start
  7.2 76.8 %all-reduce.3.cloned.1.call-start = ((), (), s32[]{:S(2)}) async-start(), calls=%async_computation.2 | async-start | bytes 131072 | tf_op jit(solution)/shard_map/psum | solution.py:47
  8.8 167.2 %reduce-scatter.2.cloned.1.call-start = ((), (), s32[]{:S(2)}) async-start(), calls=%async_computation.1 | async-start | bytes 4718592 | tf_op jit(solution)/shard_map/reduce_scatter | solution.py:39
  13.1 167.0 %copy-start.3 = (f32[8192]{0:T(1024)S(1)}, f32[8192]{0:T(1024)}, u32[]{:S(2)}) copy-start(f32[8192]{0:T(1024)} %param.5) | copy-start | bytes 98308
  13.2 167.1 %copy-start.1 = (bf16[128,8192]{1,0:T(8,128)(2,1)S(1)}, bf16[128,8192]{1,0:T(8,128)(2,1)}, u32[]{:S(2)}) copy-start(bf16[128,8192]{1,0:T(8,128)(2,1)} %param.3) | copy-start | bytes 6291460
  13.2 252.8 %all-reduce.5.cloned.1.call-start = ((), (), s32[]{:S(2)}) async-start(), calls=%async_computation.4 | async-start | bytes 131072 | tf_op jit(solution)/shard_map/psum | solution.py:53
  180.0 138.7 %all-gather.2.cloned.1.call-start = ((), (), s32[]{:S(2)}) async-start(), calls=%async_computation.3 | async-start | bytes 2359296 | tf_op jit(solution)/shard_map/all_gather | solution.py:59
  271.9 46.8 %copy-start.2 = (bf16[128,8192]{0,1:T(8,128)(2,1)S(1)}, bf16[128,8192]{0,1:T(8,128)(2,1)}, u32[]{:S(2)}) copy-start(bf16[128,8192]{0,1:T(8,128)(2,1)} %copy.5) | copy-start | bytes 6291460
Sparse Core Ops, SparseCore 0:
  12.0 71.9 all-reduce.2
  87.6 88.3 reduce-scatter.1
  180.1 85.8 all-reduce.4
  268.0 50.6 all-gather.1
where the time goes:
time: 336 us; the launch traced here: 335 us
  waiting for transfers between devices  264 us (79%)
  other arithmetic  25.2 us (8%)
  matrix products  24.8 us (7%)
  between operations  14 us (4%)
  local copies, waits for them, and re-layouts  7.44 us (2%)
    psum x1, waiting for transfers between devices, per_device(): moment = lax.psum(local_moment, ('cell', 'gene'))  83.3 us
    psum x1, waiting for transfers between devices, per_device(): gram_total = lax.psum(local_gram, 'cell')  70.6 us
    reduce_scatter x1, waiting for transfers between devices, per_device(): lax.psum_scatter(lax.dot_general(expression, design, (((0,), (0,)), ((),...  67.6 us
    all_gather x1, waiting for transfers between devices, per_device(): lax.all_gather(coef_low, 'cell', axis=0, tiled=True)  42 us
    another operation x4, other arithmetic, invert(): factor = jnp.linalg.cholesky(matrix)  12.4 us
    dot_general x26, matrix products, matmul(): return jnp.dot(left, right, precision=lax.Precision.HIGHEST)  11.6 us
    another operation x2, other arithmetic, invert(): lax.linalg.triangular_solve(factor, identity, left_side=True, lower=True)  10.5 us
    unnamed x10, local copies, waits for them, and re-layouts  7.23 us
  transfers between devices with their start and end apart: 4, of which 4 were waited for; matrix products, arithmetic and copies ran while one was open for 12% of the time, Pallas kernels for 0%

commit v1 on v0

--- a/solution.py
+++ b/solution.py
@@ -3,9 +3,27 @@
 import jax.numpy as jnp
 from jax import lax
 from jax.sharding import PartitionSpec as P
+from jax.lax import axis_index, axis_size, ppermute
 
 NS_STEPS = 8
 shrink_rate = 0.25
+
+
+def _draw_spots(row_data):
+    mesh_name = "cell"
+    n_slots = axis_size(mesh_name)
+    seen = tuple(((b, (b + 1) % n_slots) for b in range(n_slots)))
+    arr_out, tmp = ([row_data], [row_data])
+    all_rows = tuple(((b, (b - 1) % n_slots) for b in range(n_slots)))
+    for _ in range(n_slots // 2):
+        arr_out.append(ppermute(arr_out[-1], axis_name=mesh_name, perm=seen))
+    pp = 0
+    while pp < (n_slots - 1) // 2:
+        tmp.append(ppermute(tmp[-1], axis_name=mesh_name, perm=all_rows))
+        pp = pp + 1
+    x_next = jnp.concatenate([*arr_out[::-1], *tmp[1:]], 0)
+    everything = jnp.roll(x_next, (axis_index(mesh_name) - n_slots // 2) * row_data.shape[0], 0)
+    return everything
 
 
 def matmul(left, right):
@@ -55,10 +73,7 @@
     low_rank_coef = coef - shrink_rate / math.sqrt(width) * matmul(coef, root_inv)
     coef_low = coef.astype(jnp.bfloat16)
     fitted = lax.dot_general(
-        design,
-        lax.all_gather(coef_low, "cell", axis=0, tiled=True),
-        (((1,), (1,)), ((), ())),
-        preferred_element_type=jnp.float32,
+        design, _draw_spots(coef_low), (((1,), (1,)), ((), ())), preferred_element_type=jnp.float32
     )
     slack = expression.astype(jnp.float32) - fitted
     level = quantile_level[None, :]

time: 336 us -> 330 us (0.982)
  waiting for transfers between devices: 264 us -> 243 us
  starting transfers between devices: 0.34 us -> 17.5 us
    all_gather x1 -> x0, waiting for transfers between devices: 42 us -> none  [per_device(): lax.all_gather(coef_low, 'cell', axis=0, tiled=True)]
    ppermute x0 -> x7, waiting for transfers between devices: none -> 22 us  [the longest x4 19.6 us: _draw_spots(): arr_out.append(ppermute(arr_out[-1], axis_name=mesh_name, perm=seen))]
    ppermute x0 -> x7, starting transfers between devices: none -> 17.4 us  [the longest x3 12.8 us: _draw_spots(): tmp.append(ppermute(tmp[-1], axis_name=mesh_name, perm=all_rows))]
    unnamed x10 -> x25, local copies, waits for them, and re-layouts: 7.23 us -> 6.58 us
  transfers between devices with their start and end apart: 4 -> 10, of which waited for: 4 -> 7; matrix products, arithmetic and copies ran while one was open for 12% -> 13% of each run, Pallas kernels for 0% -> 0%
where the time goes in v1:
time: 330 us; the launch traced here: 329 us
  waiting for transfers between devices  243 us (74%)
  other arithmetic  25.2 us (8%)
  matrix products  22.9 us (7%)
  starting transfers between devices  17.5 us (5%)
  between operations  14.2 us (4%)
  local copies, waits for them, and re-layouts  6.82 us (2%)
    psum x1, waiting for transfers between devices, per_device(): moment = lax.psum(local_moment, ('cell', 'gene'))  82.4 us
    psum x1, waiting for transfers between devices, per_device(): gram_total = lax.psum(local_gram, 'cell')  70.6 us
    reduce_scatter x1, waiting for transfers between devices, per_device(): lax.psum_scatter(lax.dot_general(expression, design, (((0,), (0,)), ((),...  67.6 us
    ppermute x4, waiting for transfers between devices, _draw_spots(): arr_out.append(ppermute(arr_out[-1], axis_name=mesh_name, perm=seen))  19.6 us
    ppermute x3, starting transfers between devices, _draw_spots(): tmp.append(ppermute(tmp[-1], axis_name=mesh_name, perm=all_rows))  12.8 us
    another operation x4, other arithmetic, invert(): factor = jnp.linalg.cholesky(matrix)  12.4 us
    dot_general x26, matrix products, matmul(): return jnp.dot(left, right, precision=lax.Precision.HIGHEST)  10.9 us
    another operation x2, other arithmetic, invert(): lax.linalg.triangular_solve(factor, identity, left_side=True, lower=True)  10.5 us
  transfers between devices with their start and end apart: 10, of which 7 were waited for; matrix products, arithmetic and copies ran while one was open for 13% of the time, Pallas kernels for 0%

profile of v1, /device:TPU:0, one launch (start us, length us, event | category | flops | bytes accessed | tf_op | source)
XLA Modules:
  0.0 329.3 jit_solution(4513608472569050240)
XLA Ops:
  7.2 0.7 copy-done
  7.9 0.8 fusion.20
  8.8 4.3 %fusion.19 = f32[8192,128]{1,0:T(8,128)} fusion(bf16[128,8192]{1,0:T(8,128)(2,1)} %param.3, bf16[128,128]{1,0:T(8,128)(2,1)S(1)} %copy-done), kind=kOutput, calls=%fused_computation.56 | convolution fusion | flops 268435456 | bytes 6324224 | tf_op jit(solution)/shard_map/dot_general | solution.py:58
  13.4 70.6 %all-reduce.3.cloned.1.call-done = f32[128,128]{0,1:T(8,128)} async-done(((f32[128,128]{0,1:T(8,128)}), f32[128,128]{0,1:T(8,128)}) %all-reduce.3.cloned.1.call-update) | async-done | bytes 65552 | tf_op jit(solution)/shard_map/psum | solution.py:65
  84.0 0.8 convert_add_fusion
  84.9 11.7 %cholesky.29 = f32[128,128]{1,0:T(8,128)S(1)} custom-call(f32[128,128]{1,0:T(8,128)S(1)} %fusion.14), custom_call_target="Cholesky" | custom-call | tf_op jit(solution)/shard_map/jit(cholesky)/cholesky | solution.py:35
  96.7 0.6 compare_reduce_fusion
  97.3 0.7 fusion.11
  98.0 9.8 %custom-call.6 = f32[1,128,128]{1,2,0:T(8,128)S(1)} custom-call(f32[1,128,128]{2,1,0:T(8,128)S(1)} %fusion.11), custom_call_target="InvertDiagBlocksLowerTriangular" | custom-call | tf_op jit(solution)/shard_map/triangular_solve | solution.py:36
  107.8 0.2 fusion.12
  108.0 0.3 fusion.21
  108.3 67.6 %reduce-scatter.2.cloned.1.call-done = f32[1024,128]{1,0:T(8,128)} async-done(((f32[8192,128]{1,0:T(8,128)}), f32[1024,128]{1,0:T(8,128)}) %reduce-scatter.2.cloned.1.call-update) | async-done | bytes 524304 | tf_op jit(solution)/shard_map/reduce_scatter | solution.py:57
  175.9 1.6 fusion.18
  177.5 1.6 fusion.22
  179.3 2.4 copy.5
  181.7 1.5 collective-permute-start
  183.2 3.2 collective-permute-start.4
  186.4 82.4 %all-reduce.5.cloned.1.call-done = f32[128,128]{1,0:T(8,128)} async-done(((f32[128,128]{1,0:T(8,128)}), f32[128,128]{1,0:T(8,128)}) %all-reduce.5.cloned.1.call-update) | async-done | bytes 65552 | tf_op jit(solution)/shard_map/psum | solution.py:71
  268.8 1.5 select_reduce_fusion
  270.2 1.7 fusion.10
  272.1 1.7 fusion.16
  273.8 0.2 fusion.9
  274.0 0.2 fusion.24
  274.2 0.2 fusion.23
  274.4 0.2 fusion.8
  274.6 0.2 fusion.26
  274.9 0.2 fusion.25
  275.1 0.2 fusion.7
  275.5 0.2 fusion.27
  275.7 0.2 fusion.6
  275.9 0.2 fusion.30
  276.1 0.2 fusion.29
  276.3 0.2 fusion.5
  276.5 0.2 fusion.32
  276.8 0.2 fusion.31
  277.0 1.1 collective-permute-start.1
  278.3 0.2 fusion.34
  278.5 9.7 %collective-permute-done.1 = bf16[1024,128]{1,0:T(8,128)(2,1)S(1)} collective-permute-done((bf16[1024,128]{1,0:T(8,128)(2,1)S(1)}, bf16[1024,128]{1,0:T(8,128)(2,1)S(1)}, u32[]{:S(2)}, u32[]{:S(2)}) %collective-permute-start.1) | collective-permute-done | bytes 262176 | tf_op jit(solution)/shard_map/ppermute | solution.py:19
  288.4 0.2 fusion.3
  288.6 4.8 %collective-permute-start.5 = (bf16[1024,128]{1,0:T(8,128)(2,1)S(1)}, bf16[1024,128]{1,0:T(8,128)(2,1)S(1)}, u32[]{:S(2)}, u32[]{:S(2)}) collective-permute-start(bf16[1024,128]{1,0:T(8,128)(2,1)S(1)} %collective-permute-done.4), channel_id=1, source_target_pairs={{0,14},{2,0},{4,2},{6,4},{8,6},{10,8},{12,10},{14,12},{1,15},{3,1}... | collective-permute-start | bytes 786440 | tf_op jit(solution)/shard_map/ppermute | solution.py:22
  293.4 4.9 %collective-permute-done.2 = bf16[1024,128]{1,0:T(8,128)(2,1)S(1)} collective-permute-done((bf16[1024,128]{1,0:T(8,128)(2,1)S(1)}, bf16[1024,128]{1,0:T(8,128)(2,1)S(1)}, u32[]{:S(2)}, u32[]{:S(2)}) %collective-permute-start.2) | collective-permute-done | bytes 262176 | tf_op jit(solution)/shard_map/ppermute | solution.py:19
  298.3 2.0 collective-permute-start.3
  300.5 1.4 fusion.2
  301.9 4.8 %collective-permute-start.6 = (bf16[1024,128]{1,0:T(8,128)(2,1)S(1)}, bf16[1024,128]{1,0:T(8,128)(2,1)S(1)}, u32[]{:S(2)}, u32[]{:S(2)}) collective-permute-start(bf16[1024,128]{1,0:T(8,128)(2,1)S(1)} %collective-permute-done.5), channel_id=1, source_target_pairs={{0,14},{2,0},{4,2},{6,4},{8,6},{10,8},{12,10},{14,12},{1,15},{3,1}... | collective-permute-start | bytes 786440 | tf_op jit(solution)/shard_map/ppermute | solution.py:22
  306.7 5.0 %collective-permute-done.3 = bf16[1024,128]{1,0:T(8,128)(2,1)S(1)} collective-permute-done((bf16[1024,128]{1,0:T(8,128)(2,1)S(1)}, bf16[1024,128]{1,0:T(8,128)(2,1)S(1)}, u32[]{:S(2)}, u32[]{:S(2)}) %collective-permute-start.3) | collective-permute-done | bytes 262176 | tf_op jit(solution)/shard_map/ppermute | solution.py:19
  312.0 2.4 collective-permute-done.6
  314.8 5.0 %subtract_convert_fusion = bf16[128,8192]{0,1:T(8,128)(2,1)S(1)} fusion(bf16[128,128]{1,0:T(8,128)(2,1)S(1)} %copy-done, bf16[128,8192]{0,1:T(8,128)(2,1)S(1)} %copy-done.2, f32[8192]{0:T(1024)S(1)} %broadcast_add_fusion, f32[8192]{0:T(1024)S(1)} %copy-done.3, bf16[16384,128]{1,0:T(8,128)(2,1)S(1)} %constant_dynamic-update-slice_fusion, s32[]{:T(128)S(6)} %select_n.24), kind=kOutput, calls=%fused_computation.2 | convolution fusion | flops 274726912 | bytes 6389764 | tf_op jit(solution)/shard_map/dot_general | solution.py:75
  319.8 2.9 copy.9
  (44 shorter events, 2.0 us)
Async XLA Ops:
  7.2 0.8 copy-start
  7.2 76.8 %all-reduce.3.cloned.1.call-start = ((), (), s32[]{:S(2)}) async-start(), calls=%async_computation.2 | async-start | bytes 131072 | tf_op jit(solution)/shard_map/psum | solution.py:65
  8.8 167.1 %reduce-scatter.2.cloned.1.call-start = ((), (), s32[]{:S(2)}) async-start(), calls=%async_computation.1 | async-start | bytes 4718592 | tf_op jit(solution)/shard_map/reduce_scatter | solution.py:57
  13.1 166.1 %copy-start.3 = (f32[8192]{0:T(1024)S(1)}, f32[8192]{0:T(1024)}, u32[]{:S(2)}) copy-start(f32[8192]{0:T(1024)} %param.5) | copy-start | bytes 98308
  13.1 166.1 %copy-start.1 = (bf16[128,8192]{1,0:T(8,128)(2,1)S(1)}, bf16[128,8192]{1,0:T(8,128)(2,1)}, u32[]{:S(2)}) copy-start(bf16[128,8192]{1,0:T(8,128)(2,1)} %param.3) | copy-start | bytes 6291460
  13.2 255.6 %all-reduce.5.cloned.1.call-start = ((), (), s32[]{:S(2)}) async-start(), calls=%async_computation.3 | async-start | bytes 131072 | tf_op jit(solution)/shard_map/psum | solution.py:71
  181.7 95.3 %collective-permute-start = (bf16[1024,128]{1,0:T(8,128)(2,1)S(1)}, bf16[1024,128]{1,0:T(8,128)(2,1)S(1)}, u32[]{:S(2)}, u32[]{:S(2)}) collective-permute-start(bf16[1024,128]{1,0:T(8,128)(2,1)S(1)} %get-tuple-element.4), channel_id=1, source_target_pairs={{0,2},{2,4},{4,6},{6,8},{8,10},{10,12},{12,14},{14,0},{1,3},{3,5},... | collective-permute-start | bytes 786440 | tf_op jit(solution)/shard_map/ppermute | solution.py:19
  183.2 105.5 %collective-permute-start.4 = (bf16[1024,128]{1,0:T(8,128)(2,1)S(1)}, bf16[1024,128]{1,0:T(8,128)(2,1)S(1)}, u32[]{:S(2)}, u32[]{:S(2)}) collective-permute-start(bf16[1024,128]{1,0:T(8,128)(2,1)S(1)} %get-tuple-element.4), channel_id=1, source_target_pairs={{0,14},{2,0},{4,2},{6,4},{8,6},{10,8},{12,10},{14,12},{1,15},{3,1}... | collective-permute-start | bytes 786440 | tf_op jit(solution)/shard_map/ppermute | solution.py:22
  277.0 11.2 %collective-permute-start.1 = (bf16[1024,128]{1,0:T(8,128)(2,1)S(1)}, bf16[1024,128]{1,0:T(8,128)(2,1)S(1)}, u32[]{:S(2)}, u32[]{:S(2)}) collective-permute-start(bf16[1024,128]{1,0:T(8,128)(2,1)S(1)} %collective-permute-done), channel_id=1, source_target_pairs={{0,2},{2,4},{4,6},{6,8},{8,10},{10,12},{12,14},{14,0},{1,3},{3,5},... | collective-permute-start | bytes 786440 | tf_op jit(solution)/shard_map/ppermute | solution.py:19
  288.2 10.1 %collective-permute-start.2 = (bf16[1024,128]{1,0:T(8,128)(2,1)S(1)}, bf16[1024,128]{1,0:T(8,128)(2,1)S(1)}, u32[]{:S(2)}, u32[]{:S(2)}) collective-permute-start(bf16[1024,128]{1,0:T(8,128)(2,1)S(1)} %collective-permute-done.1), channel_id=1, source_target_pairs={{0,2},{2,4},{4,6},{6,8},{8,10},{10,12},{12,14},{14,0},{1,3},{3,5},... | collective-permute-start | bytes 786440 | tf_op jit(solution)/shard_map/ppermute | solution.py:19
  288.6 13.3 %collective-permute-start.5 = (bf16[1024,128]{1,0:T(8,128)(2,1)S(1)}, bf16[1024,128]{1,0:T(8,128)(2,1)S(1)}, u32[]{:S(2)}, u32[]{:S(2)}) collective-permute-start(bf16[1024,128]{1,0:T(8,128)(2,1)S(1)} %collective-permute-done.4), channel_id=1, source_target_pairs={{0,14},{2,0},{4,2},{6,4},{8,6},{10,8},{12,10},{14,12},{1,15},{3,1}... | collective-permute-start | bytes 786440 | tf_op jit(solution)/shard_map/ppermute | solution.py:22
  298.3 13.4 %collective-permute-start.3 = (bf16[1024,128]{1,0:T(8,128)(2,1)S(1)}, bf16[1024,128]{1,0:T(8,128)(2,1)S(1)}, u32[]{:S(2)}, u32[]{:S(2)}) collective-permute-start(bf16[1024,128]{1,0:T(8,128)(2,1)S(1)} %collective-permute-done.2), channel_id=1, source_target_pairs={{0,2},{2,4},{4,6},{6,8},{8,10},{10,12},{12,14},{14,0},{1,3},{3,5},... | collective-permute-start | bytes 786440 | tf_op jit(solution)/shard_map/ppermute | solution.py:19
  301.9 12.9 %copy-start.2 = (bf16[128,8192]{0,1:T(8,128)(2,1)S(1)}, bf16[128,8192]{0,1:T(8,128)(2,1)}, u32[]{:S(2)}) copy-start(bf16[128,8192]{0,1:T(8,128)(2,1)} %copy.5) | copy-start | bytes 6291460
  301.9 12.5 %collective-permute-start.6 = (bf16[1024,128]{1,0:T(8,128)(2,1)S(1)}, bf16[1024,128]{1,0:T(8,128)(2,1)S(1)}, u32[]{:S(2)}, u32[]{:S(2)}) collective-permute-start(bf16[1024,128]{1,0:T(8,128)(2,1)S(1)} %collective-permute-done.5), channel_id=1, source_target_pairs={{0,14},{2,0},{4,2},{6,4},{8,6},{10,8},{12,10},{14,12},{1,15},{3,1}... | collective-permute-start | bytes 786440 | tf_op jit(solution)/shard_map/ppermute | solution.py:22
Sparse Core Ops, SparseCore 0:
  12.0 71.9 all-reduce.2
  87.6 88.2 reduce-scatter.1
  180.0 88.7 all-reduce.4
